TPU v7x, 256 devices: a whole 4x4x8 slice. The times are simulated.
256 devices in a mesh: req: 32 (over y, z), tp: 8 (over x, core).
Axes of the slice: x: 4, y: 4, z: 8, core: 2. Of those that a mesh axis runs over, the one named last changes fastest.
Arguments:
- tokens: bfloat16 [32768, 1792], P(('req', 'tp')), may hold values from -6 to 6
- norm_gain: float32 [1792], replicated, may hold values from 0.25 to 1.75
- ffn_gain: float32 [1792], replicated, may hold values from 0.25 to 1.75
- mix_weight: bfloat16 [1792, 4, 1792], P('req', None, 'tp'), may hold values from -0.125 to 0.125
- out_weight: bfloat16 [1792, 1792], P('tp', 'req'), may hold values from -0.125 to 0.125
- ffn_weight: bfloat16 [1792, 2, 7168], P('req', None, 'tp'), may hold values from -0.125 to 0.125
- down_weight: bfloat16 [7168, 1792], P('tp', 'req'), may hold values from -0.0625 to 0.0625
- conv_taps: float32 [3, 1792], P(None, 'tp'), may hold values from -3 to 3
- past_cache: bfloat16 [32, 2, 64, 1792], P('req', None, None, 'tp'), may hold values from -210 to 210
- cached_len: int32 [32], P('req'), may hold values from 0 to 8192, as said below
Outputs:
- layer_out: bfloat16 [32768, 1792], P(('req', 'tp'))
- new_cache: bfloat16 [32, 2, 64, 1792], P('req', None, None, 'tp')
Inputs may be any that keep to these rules, and one draw needn't show every extreme that they name: `cached_len`: one request has exactly 8192 cached positions and another fewer than 64.
All inputs are finite; a program needn't handle non-finite values.
Results may differ from a plain program's by a relative error of at most 0.02.
Values may be sent and summed in bfloat16 or wider, within the bound.
No kernel may reach another device: no remote copies, remote signals or barrier semaphores. Data moves between devices by JAX's collectives and lax.ppermute only.
A program may use at most 64 MiB of HBM per device.

v0:
```python
import math
import jax
import jax.numpy as jnp
from jax import lax
from jax.sharding import PartitionSpec as P

HD = 112
WIN = 64


def normed(row_vals, gain):
    floats = row_vals.astype(jnp.float32)
    scaled = floats * lax.rsqrt(jnp.mean(floats * floats, axis=-1, keepdims=True) + 1e-05)
    return (scaled * gain).astype(jnp.bfloat16)


def window_attend(queries, key_rows, value_rows, length, window):
    row_count, head_count, head_size = queries.shape
    nb = row_count // window
    score_scale = 1.0 / math.sqrt(head_size)
    qb = queries.reshape(nb, window, head_count, head_size)

    def blocks(rows):
        lo = rows[:row_count].reshape(nb, window, head_count, head_size)
        hi = rows[window:].reshape(nb, window, head_count, head_size)
        return jnp.concatenate([lo, hi], axis=1)

    kb = blocks(key_rows)
    vb = blocks(value_rows)
    scores = jnp.einsum("bqhd,bkhd->bhqk", qb, kb, preferred_element_type=jnp.float32) * score_scale
    i = jnp.arange(window, dtype=jnp.int32)[:, None]
    j = jnp.arange(2 * window, dtype=jnp.int32)[None, :]
    b = jnp.arange(nb, dtype=jnp.int32)[:, None, None]
    usable = (j > i)[None] & (j <= i + window)[None] & (b * window + j >= window - length)
    scores = jnp.where(usable[:, None], scores, -1e30)
    row_max = jnp.max(scores, axis=-1, keepdims=True)
    exponent = jnp.exp(scores - row_max)
    weights = (exponent / jnp.sum(exponent, axis=-1, keepdims=True)).astype(jnp.bfloat16)
    out = jnp.einsum("bhqk,bkhd->bqhd", weights, vb, preferred_element_type=jnp.float32)
    return out.reshape(row_count, head_count, head_size)


def mix_request(projected, cache_rows, length, tap_table, window, head_size):
    row_count, feat_width = (projected.shape[0], projected.shape[2])
    time_order = (length + jnp.arange(window, dtype=jnp.int32)) % window
    earlier = cache_rows[:, time_order]
    key_rows = jnp.concatenate([earlier[0], projected[:, 1]], axis=0)
    value_rows = jnp.concatenate([earlier[1], projected[:, 2]], axis=0)
    head_count = feat_width // head_size
    attended = window_attend(
        projected[:, 0].reshape(row_count, head_count, head_size),
        key_rows.reshape(-1, head_count, head_size),
        value_rows.reshape(-1, head_count, head_size),
        length,
        window,
    ).reshape(row_count, feat_width)
    positions = jnp.arange(window + row_count, dtype=jnp.int32)
    alive_mask = (positions >= window - length)[:, None]
    masked_values = jnp.where(alive_mask, value_rows.astype(jnp.float32), jnp.float32(0.0))
    tap_count = tap_table.shape[0]
    convolved = jnp.zeros((row_count, feat_width), jnp.float32)
    for tap_index in range(tap_count):
        begin_row = window - (tap_count - 1) + tap_index
        convolved = (
            convolved + tap_table[tap_index] * masked_values[begin_row : begin_row + row_count]
        )
    mixed_heads = (attended + projected[:, 3].astype(jnp.float32) * convolved).astype(jnp.bfloat16)
    slot_source = (
        row_count - window + (jnp.arange(window, dtype=jnp.int32) - length - row_count) % window
    )
    renewed = jnp.stack([projected[:, 1], projected[:, 2]])[:, slot_source]
    return (mixed_heads, renewed)


def gather_weights(mix_weight, out_weight, ffn_weight, down_weight):
    rows = mix_weight.shape[0]
    pieces = [
        mix_weight.reshape(rows, -1),
        ffn_weight.reshape(rows, -1),
        down_weight.T,
        out_weight.T,
    ]
    widths = [p.shape[1] for p in pieces]
    got = lax.all_gather(jnp.concatenate(pieces, axis=1), "req", axis=0, tiled=True)
    parts = []
    start = 0
    for w in widths:
        parts.append(got[:, start : start + w])
        start += w
    return parts


def tp_gather(x):
    n = lax.axis_size("tp")
    return lax.all_to_all(jnp.tile(x, (n, 1)), "tp", 0, 0, tiled=True)


def tp_sum_scatter(x):
    n = lax.axis_size("tp")
    got = lax.all_to_all(x, "tp", 0, 0, tiled=True)
    return got.reshape((n, -1) + x.shape[1:]).astype(jnp.float32).sum(axis=0)


def local(
    tokens,
    norm_gain,
    ffn_gain,
    mix_weight,
    out_weight,
    ffn_weight,
    down_weight,
    conv_taps,
    past_cache,
    cached_len,
):
    feat_width = mix_weight.shape[2]
    ffn_width = ffn_weight.shape[2]
    mix_all, ffn_all, down_t, out_t = gather_weights(
        mix_weight, out_weight, ffn_weight, down_weight
    )
    normed_all = tp_gather(normed(tokens, norm_gain))
    row_total = normed_all.shape[0]
    projected = jnp.dot(normed_all, mix_all, preferred_element_type=jnp.float32)
    projected = projected.astype(jnp.bfloat16).reshape(row_total, 4, feat_width)
    mixed_heads, renewed = mix_request(projected, past_cache[0], cached_len[0], conv_taps, WIN, HD)
    attn_full = lax.dot_general(
        mixed_heads, out_t, (((1,), (1,)), ((), ())), preferred_element_type=jnp.float32
    )
    attn_part = tp_sum_scatter(attn_full.astype(jnp.bfloat16))
    residual = (tokens.astype(jnp.float32) + attn_part).astype(jnp.bfloat16)
    ffn_in = tp_gather(normed(residual, ffn_gain))
    gate_up = jnp.dot(ffn_in, ffn_all, preferred_element_type=jnp.float32)
    activated = (jax.nn.silu(gate_up[:, :ffn_width]) * gate_up[:, ffn_width:]).astype(jnp.bfloat16)
    ffn_full = lax.dot_general(
        activated, down_t, (((1,), (1,)), ((), ())), preferred_element_type=jnp.float32
    )
    ffn_part = tp_sum_scatter(ffn_full.astype(jnp.bfloat16))
    layer_out = (residual.astype(jnp.float32) + ffn_part).astype(jnp.bfloat16)
    return (layer_out, renewed[None])


def solution(mesh):
    in_specs = (
        P(("req", "tp"), None),
        P(),
        P(),
        P("req", None, "tp"),
        P("tp", "req"),
        P("req", None, "tp"),
        P("tp", "req"),
        P(None, "tp"),
        P("req", None, None, "tp"),
        P("req"),
    )
    out_specs = (P(("req", "tp"), None), P("req", None, None, "tp"))
    return jax.shard_map(local, mesh=mesh, in_specs=in_specs, out_specs=out_specs, check_vma=False)
```

profile of v0, /device:TPU:1, one launch (start us, length us, event | category | flops | bytes accessed | tf_op | source)
XLA Modules:
  0.0 342.7 jit_solution(4850070380336900980)
XLA Ops:
  7.2 1.0 reshape.257
  8.3 1.0 copy.55
  9.2 1.7 pad_maximum_fusion.3
  11.0 1.2 fusion.20
  12.2 1.2 fusion.22
  13.4 2.0 tile.4
  15.4 7.8 %all-to-all-start = ((bf16[8,128,1792]{2,1,0:T(8,128)(2,1)}), bf16[8,128,1792]{2,1,0:T(8,128)(2,1)}, u32[]{:S(2)}, u32[]{:S(2)}) async-start(bf16[8,128,1792]{2,1,0:T(8,128)(2,1)} %tile.4), calls=%async_computation | async-start | bytes 7340032 | tf_op jit(solution)/shard_map/all_to_all | solution.py:95
  25.2 41.3 %all-to-all-done = bf16[8,128,1792]{2,1,0:T(8,128)(2,1)} async-done(((bf16[8,128,1792]{2,1,0:T(8,128)(2,1)}), bf16[8,128,1792]{2,1,0:T(8,128)(2,1)}, u32[]{:S(2)}, u32[]{:S(2)}) %all-to-all-start) | async-done | bytes 3670048 | tf_op jit(solution)/shard_map/all_to_all | solution.py:95
  66.5 73.7 %all-gather.2.cloned.1.call-done = bf16[1792,3808]{1,0:T(8,128)(2,1)} async-done(((bf16[56,3808]{1,0:T(8,128)(2,1)}), bf16[1792,3808]{1,0:T(8,128)(2,1)}) %all-gather.2.cloned.1.call-update) | async-done | bytes 13647888 | tf_op jit(solution)/shard_map/all_gather | solution.py:84
  140.2 6.6 %fusion.9 = bf16[1024,896]{0,1:T(8,128)(2,1)S(1)} fusion(bf16[1024,1792]{1,0:T(8,128)(2,1)} %bitcast.4, bf16[1792,3808]{1,0:T(8,128)(2,1)} %all-gather.2.cloned.1.call-done), kind=kOutput, calls=%fused_computation.15 | convolution fusion | flops 3289251840 | bytes 8716288 | tf_op jit(solution)/shard_map/dot_general | solution.py:123
  146.7 1.2 slice_bitcast_fusion
  149.0 1.5 reshape.281
  150.5 1.7 reshape.283
  152.5 2.5 fusion.63
  155.0 3.0 fusion.14
  158.9 1.2 copy.28
  160.1 1.2 copy.29
  161.4 1.0 copy.54
  162.4 6.3 %convolution_bitcast_fusion = f32[16,64,2,112]{3,1,2,0:T(8,128)S(1)} fusion(bf16[16,64,2,112]{1,3,2,0:T(8,128)(2,1)} %copy.29, bf16[16,64,2,112]{1,3,2,0:T(8,128)(2,1)} %copy.28, f32[16,2,64]{2,1,0:T(2,128)S(1)} %fusion.63, f32[16,2,64,128]{3,2,1,0:T(8,128)} %fusion.14), kind=kOutput, calls=%fused_computation.26 | convolution fusion | flops 61343872 | bytes 2891776 | tf_op jit(solution)/shard_map/bhqk,bkhd->bqhd/dot_general | solution.py:39
  168.6 0.8 copy.37
  170.3 2.9 convolution_convert_fusion.1
  173.2 48.7 %all_to_all.36 = bf16[8,128,1792]{2,1,0:T(8,128)(2,1)S(1)} all-to-all(bf16[8,128,1792]{2,1,0:T(8,128)(2,1)S(1)} %bitcast.59), channel_id=1, replica_groups=mesh['req'=32,'tp'=8] {'tp'}, dimensions={0} | all-to-all | bytes 7340032 | tf_op jit(solution)/shard_map/all_to_all | solution.py:100
  223.6 47.2 %all_to_all.37 = bf16[8,128,1792]{2,1,0:T(8,128)(2,1)S(1)} all-to-all(bf16[8,128,1792]{2,1,0:T(8,128)(2,1)S(1)} %tile.5), channel_id=1, replica_groups=mesh['req'=32,'tp'=8] {'tp'}, dimensions={0} | all-to-all | bytes 7340032 | tf_op jit(solution)/shard_map/all_to_all | solution.py:95
  270.8 6.8 %fusion.1 = f32[1024,1792]{1,0:T(8,128)S(1)} fusion(bf16[1024,1792]{1,0:T(8,128)(2,1)S(1)} %bitcast.60, bf16[1792,3808]{1,0:T(8,128)(2,1)S(1)} %bitcast.76), kind=kOutput, calls=%fused_computation.5 | convolution fusion | flops 6576668672 | bytes 17432576 | tf_op jit(solution)/shard_map/dot_general | solution.py:132
  277.7 6.0 %convolution_convert_fusion = bf16[1024,1792]{1,0:T(8,128)(2,1)} fusion(bf16[1792,3808]{1,0:T(8,128)(2,1)S(1)} %bitcast.76, f32[1024,1792]{1,0:T(8,128)S(1)} %fusion.1), kind=kOutput, calls=%fused_computation.7 | convolution fusion | flops 3295674368 | bytes 14221312 | tf_op jit(solution)/shard_map/dot_general | solution.py:134
  283.6 5.4 %all-to-all-start.3 = ((bf16[8,128,1792]{2,1,0:T(8,128)(2,1)}), bf16[8,128,1792]{2,1,0:T(8,128)(2,1)}, u32[]{:S(2)}, u32[]{:S(2)}) async-start(bf16[8,128,1792]{2,1,0:T(8,128)(2,1)} %bitcast.58), calls=%async_computation.3 | async-start | bytes 7340032 | tf_op jit(solution)/shard_map/all_to_all | solution.py:100
  289.1 0.9 copy.40
  289.9 0.8 copy.41
  290.7 2.6 pad_maximum_fusion
  294.7 37.6 %all-to-all-done.3 = bf16[8,128,1792]{2,1,0:T(8,128)(2,1)} async-done(((bf16[8,128,1792]{2,1,0:T(8,128)(2,1)}), bf16[8,128,1792]{2,1,0:T(8,128)(2,1)}, u32[]{:S(2)}, u32[]{:S(2)}) %all-to-all-start.3) | async-done | bytes 3670048 | tf_op jit(solution)/shard_map/all_to_all | solution.py:100
  332.4 2.6 convert_reduce_fusion
  335.0 0.8 fusion.27
  (56 shorter events, 7.3 us)
Async XLA Ops:
  7.2 133.0 %all-gather.2.cloned.1.call-start = ((), (), s32[]{:S(2)}) async-start(), calls=%async_computation.4 | async-start | bytes 14192640 | tf_op jit(solution)/shard_map/all_gather | solution.py:84
  15.4 8.4 %copy-start.3 = (bf16[1,2,64,224]{3,2,1,0:T(8,128)(2,1)S(1)}, bf16[1,2,64,224]{3,2,1,0:T(8,128)(2,1)}, u32[]{:S(2)}) copy-start(bf16[1,2,64,224]{3,2,1,0:T(8,128)(2,1)} %param.18) | copy-start | bytes 172036
  15.4 9.6 %copy-start.5 = (f32[3,224]{1,0:T(4,128)S(1)}, f32[3,224]{1,0:T(4,128)}, u32[]{:S(2)}) copy-start(f32[3,224]{1,0:T(4,128)} %param.17) | copy-start | bytes 8068
  15.4 51.1 %all-to-all-start = ((bf16[8,128,1792]{2,1,0:T(8,128)(2,1)}), bf16[8,128,1792]{2,1,0:T(8,128)(2,1)}, u32[]{:S(2)}, u32[]{:S(2)}) async-start(bf16[8,128,1792]{2,1,0:T(8,128)(2,1)} %tile.4), calls=%async_computation | async-start | bytes 7340032 | tf_op jit(solution)/shard_map/all_to_all | solution.py:95
  152.4 5.5 %copy-start.2 = (bf16[1024,1,224]{0,2,1:T(8,128)(2,1)S(1)}, bf16[1024,1,224]{0,2,1:T(8,128)(2,1)}, u32[]{:S(2)}) copy-start(bf16[1024,1,224]{0,2,1:T(8,128)(2,1)} %get-tuple-element.10) | copy-start | bytes 1376260
  158.0 3.4 copy-start.1
  170.3 100.5 %slice-start = ((s8[13762560]{0:T(1024)(128)(4,1)}), s8[4194304]{0:T(1024)(128)(4,1)S(1)}, s32[]{:S(2)}) async-start(s8[13762560]{0:T(1024)(128)(4,1)} %bitcast.75), calls=%async_computation.5 | async-start | bytes 8388608
  170.3 100.5 %slice-start.1 = ((s8[13762560]{0:T(1024)(128)(4,1)}), s8[4194304]{0:T(1024)(128)(4,1)S(1)}, s32[]{:S(2)}) async-start(s8[13762560]{0:T(1024)(128)(4,1)} %bitcast.75), calls=%async_computation.6 | async-start | bytes 8388608
  221.9 1.0 copy-start
  221.9 1.2 copy-start.4
  221.9 48.9 %slice-start.2 = ((s8[13762560]{0:T(1024)(128)(4,1)}), s8[4194304]{0:T(1024)(128)(4,1)S(1)}, s32[]{:S(2)}) async-start(s8[13762560]{0:T(1024)(128)(4,1)} %bitcast.75), calls=%async_computation.7 | async-start | bytes 8388608
  223.3 47.5 %slice-start.3 = ((s8[13762560]{0:T(1024)(128)(4,1)}), s8[1179648]{0:T(1024)(128)(4,1)S(1)}, s32[]{:S(2)}) async-start(s8[13762560]{0:T(1024)(128)(4,1)} %bitcast.75), calls=%async_computation.8 | async-start | bytes 2359296
  283.6 48.7 %all-to-all-start.3 = ((bf16[8,128,1792]{2,1,0:T(8,128)(2,1)}), bf16[8,128,1792]{2,1,0:T(8,128)(2,1)}, u32[]{:S(2)}, u32[]{:S(2)}) async-start(bf16[8,128,1792]{2,1,0:T(8,128)(2,1)} %bitcast.58), calls=%async_computation.3 | async-start | bytes 7340032 | tf_op jit(solution)/shard_map/all_to_all | solution.py:100
Sparse Core Ops, SparseCore 0:
  11.2 128.9 all-gather.1
where the time goes:
time: 343 us
  waiting for transfers between devices  153 us (45%)
  blocking collectives  95.9 us (28%)
  matrix products  34 us (10%)
  local copies, waits for them, and re-layouts  20 us (6%)
  between operations  15 us (4%)
  starting transfers between devices  13.2 us (4%)
  other arithmetic  11.9 us (3%)
    all_gather x1, waiting for transfers between devices, gather_weights(): lax.all_gather(jnp.concatenate(pieces, axis=1), 'req', axis=0, tiled=True)  73.7 us
    all_to_all x1, blocking collectives, tp_sum_scatter(): got = lax.all_to_all(x, 'tp', 0, 0, tiled=True)  48.7 us
    all_to_all x1, blocking collectives, tp_gather(): return lax.all_to_all(jnp.tile(x, (n, 1)), 'tp', 0, 0, tiled=True)  47.2 us
    all_to_all x1, waiting for transfers between devices, tp_gather(): return lax.all_to_all(jnp.tile(x, (n, 1)), 'tp', 0, 0, tiled=True)  41.3 us
    all_to_all x1, waiting for transfers between devices, tp_sum_scatter(): got = lax.all_to_all(x, 'tp', 0, 0, tiled=True)  37.6 us
    all_to_all x1, starting transfers between devices, tp_gather(): return lax.all_to_all(jnp.tile(x, (n, 1)), 'tp', 0, 0, tiled=True)  7.76 us
  transfers between devices with their start and end apart: 3, of which 3 were waited for; matrix products, arithmetic and copies ran while one was open for 3% of the time, Pallas kernels for 0%

commit v1 on v0

--- a/solution.py
+++ b/solution.py
@@ -81,7 +81,12 @@
         out_weight.T,
     ]
     widths = [p.shape[1] for p in pieces]
-    got = lax.all_gather(jnp.concatenate(pieces, axis=1), "req", axis=0, tiled=True)
+    got = jnp.concatenate(
+        lax.all_to_all(
+            jnp.stack([jnp.concatenate(pieces, axis=1)] * lax.axis_size("req")), "req", 0, 0
+        ),
+        axis=0,
+    )
     parts = []
     start = 0
     for w in widths:

time: 343 us -> 599 us (1.75)
  the two profiles are of different devices: /device:TPU:1 before, /device:TPU:184 now
where the time goes in v1:
time: 599 us; the launch traced here: 598 us
  waiting for transfers between devices  407 us (68%)
  blocking collectives  95 us (16%)
  matrix products  36.6 us (6%)
  local copies, waits for them, and re-layouts  26.3 us (4%)
  starting transfers between devices  18.7 us (3%)
  other arithmetic  12.3 us (2%)
    all_to_all x1, waiting for transfers between devices, gather_weights(): lax.all_to_all(jnp.stack([jnp.concatenate(pieces, axis=1)] * lax.axis_siz...  327 us
    all_to_all x1, blocking collectives, tp_sum_scatter(): got = lax.all_to_all(x, 'tp', 0, 0, tiled=True)  47.9 us
    all_to_all x1, blocking collectives, tp_gather(): return lax.all_to_all(jnp.tile(x, (n, 1)), 'tp', 0, 0, tiled=True)  47.1 us
    all_to_all x1, waiting for transfers between devices, tp_gather(): return lax.all_to_all(jnp.tile(x, (n, 1)), 'tp', 0, 0, tiled=True)  43.8 us
    all_to_all x1, waiting for transfers between devices, tp_sum_scatter(): got = lax.all_to_all(x, 'tp', 0, 0, tiled=True)  36.3 us
  transfers between devices with their start and end apart: 3, of which 3 were waited for; matrix products, arithmetic and copies ran while one was open for 2% of the time, Pallas kernels for 0%

profile of v1, /device:TPU:184, one launch (start us, length us, event | category | flops | bytes accessed | tf_op | source)
XLA Modules:
  0.0 598.0 jit_solution(1000163553284832044)
XLA Ops:
  0.6 1.2 fusion.20
  1.8 1.2 fusion.22
  3.0 2.0 tile.4
  5.1 4.6 all-to-all-start
  10.0 43.8 %all-to-all-done = bf16[8,128,1792]{2,1,0:T(8,128)(2,1)} async-done(((bf16[8,128,1792]{2,1,0:T(8,128)(2,1)}), bf16[8,128,1792]{2,1,0:T(8,128)(2,1)}, u32[]{:S(2)}, u32[]{:S(2)}) %all-to-all-start) | async-done | bytes 3670048 | tf_op jit(solution)/shard_map/all_to_all | solution.py:100
  53.8 5.9 stack.4
  59.6 9.5 %all-to-all-start.1 = ((bf16[32,56,3808]{2,1,0:T(8,128)(2,1)}), bf16[32,56,3808]{2,1,0:T(8,128)(2,1)}, u32[]{:S(2)}, u32[]{:S(2)}) async-start(bf16[32,56,3808]{2,1,0:T(8,128)(2,1)} %stack.4), calls=%async_computation.1 | async-start | bytes 27525120 | tf_op jit(solution)/shard_map/all_to_all | solution.py:85
  71.7 327.3 %all-to-all-done.1 = bf16[32,56,3808]{2,1,0:T(8,128)(2,1)} async-done(((bf16[32,56,3808]{2,1,0:T(8,128)(2,1)}), bf16[32,56,3808]{2,1,0:T(8,128)(2,1)}, u32[]{:S(2)}, u32[]{:S(2)}) %all-to-all-start.1) | async-done | bytes 13647904 | tf_op jit(solution)/shard_map/all_to_all | solution.py:85
  398.9 6.6 %fusion.9 = bf16[1024,896]{0,1:T(8,128)(2,1)S(1)} fusion(bf16[1024,1792]{1,0:T(8,128)(2,1)} %bitcast.4, bf16[1792,3808]{1,0:T(8,128)(2,1)} %bitcast.7), kind=kOutput, calls=%fused_computation.15 | convolution fusion | flops 3289251840 | bytes 8716288 | tf_op jit(solution)/shard_map/dot_general | solution.py:128
  405.5 1.3 slice_bitcast_fusion
  407.9 1.7 reshape.289
  409.8 1.7 reshape.287
  411.5 1.8 fusion.14
  413.3 1.9 fusion.63
  415.2 1.2 copy.53
  417.2 1.3 copy.28
  419.2 6.0 %convolution_bitcast_fusion = f32[16,64,2,112]{3,1,2,0:T(8,128)S(1)} fusion(bf16[16,64,2,112]{1,3,2,0:T(8,128)(2,1)S(1)} %copy.29, bf16[16,64,2,112]{1,3,2,0:T(8,128)(2,1)} %copy.28, f32[16,2,64]{2,1,0:T(2,128)} %fusion.63, f32[16,2,64,128]{3,2,1,0:T(8,128)} %fusion.14), kind=kOutput, calls=%fused_computation.26 | convolution fusion | flops 61343872 | bytes 2891776 | tf_op jit(solution)/shard_map/bhqk,bkhd->bqhd/dot_general | solution.py:39
  425.2 0.8 copy.37
  426.0 1.6 reshape_reshape.3
  427.6 1.0 convert_select_fusion
  428.8 2.9 convolution_convert_fusion.1
  431.7 47.9 %all_to_all.41 = bf16[8,128,1792]{2,1,0:T(8,128)(2,1)S(1)} all-to-all(bf16[8,128,1792]{2,1,0:T(8,128)(2,1)S(1)} %bitcast.60), channel_id=1, replica_groups=mesh['req'=32,'tp'=8] {'tp'}, dimensions={0} | all-to-all | bytes 7340032 | tf_op jit(solution)/shard_map/all_to_all | solution.py:105
  481.3 47.1 %all_to_all.42 = bf16[8,128,1792]{2,1,0:T(8,128)(2,1)S(1)} all-to-all(bf16[8,128,1792]{2,1,0:T(8,128)(2,1)S(1)} %tile.5), channel_id=1, replica_groups=mesh['req'=32,'tp'=8] {'tp'}, dimensions={0} | all-to-all | bytes 7340032 | tf_op jit(solution)/shard_map/all_to_all | solution.py:100
  528.4 9.6 %fusion.1 = f32[1024,1792]{1,0:T(8,128)S(1)} fusion(bf16[1024,1792]{1,0:T(8,128)(2,1)S(1)} %bitcast.61, bf16[1792,3808]{1,0:T(8,128)(2,1)} %bitcast.7), kind=kOutput, calls=%fused_computation.5 | convolution fusion | flops 6576668672 | bytes 17432576 | tf_op jit(solution)/shard_map/dot_general | solution.py:137
  538.1 7.8 %convolution_convert_fusion = bf16[1024,1792]{1,0:T(8,128)(2,1)} fusion(bf16[1792,3808]{1,0:T(8,128)(2,1)} %bitcast.7, f32[1024,1792]{1,0:T(8,128)S(1)} %fusion.1), kind=kOutput, calls=%fused_computation.7 | convolution fusion | flops 3295674368 | bytes 14221312 | tf_op jit(solution)/shard_map/dot_general | solution.py:139
  545.9 4.6 all-to-all-start.4
  551.4 0.9 copy.40
  552.2 3.4 pad_maximum_fusion
  555.6 1.9 gather_fusion.1
  558.2 36.3 %all-to-all-done.4 = bf16[8,128,1792]{2,1,0:T(8,128)(2,1)} async-done(((bf16[8,128,1792]{2,1,0:T(8,128)(2,1)}), bf16[8,128,1792]{2,1,0:T(8,128)(2,1)}, u32[]{:S(2)}, u32[]{:S(2)}) %all-to-all-start.4) | async-done | bytes 3670048 | tf_op jit(solution)/shard_map/all_to_all | solution.py:105
  594.6 2.6 convert_reduce_fusion
  597.2 0.8 fusion.27
  (57 shorter events, 8.1 us)
Async XLA Ops:
  5.1 4.7 copy-start.3
  5.1 4.7 copy-start.4
  5.1 4.8 copy-start.5
  5.1 4.9 copy-start.7
  5.1 48.7 %all-to-all-start = ((bf16[8,128,1792]{2,1,0:T(8,128)(2,1)}), bf16[8,128,1792]{2,1,0:T(8,128)(2,1)}, u32[]{:S(2)}, u32[]{:S(2)}) async-start(bf16[8,128,1792]{2,1,0:T(8,128)(2,1)} %tile.4), calls=%async_computation | async-start | bytes 7340032 | tf_op jit(solution)/shard_map/all_to_all | solution.py:100
  59.6 10.1 %copy-start.6 = (bf16[1,2,64,224]{3,2,1,0:T(8,128)(2,1)S(1)}, bf16[1,2,64,224]{3,2,1,0:T(8,128)(2,1)}, u32[]{:S(2)}) copy-start(bf16[1,2,64,224]{3,2,1,0:T(8,128)(2,1)} %param.18) | copy-start | bytes 172036
  59.6 11.9 %copy-start.9 = (f32[3,224]{1,0:T(4,128)S(1)}, f32[3,224]{1,0:T(4,128)}, u32[]{:S(2)}) copy-start(f32[3,224]{1,0:T(4,128)} %param.17) | copy-start | bytes 8068
  59.6 339.3 %all-to-all-start.1 = ((bf16[32,56,3808]{2,1,0:T(8,128)(2,1)}), bf16[32,56,3808]{2,1,0:T(8,128)(2,1)}, u32[]{:S(2)}, u32[]{:S(2)}) async-start(bf16[32,56,3808]{2,1,0:T(8,128)(2,1)} %stack.4), calls=%async_computation.1 | async-start | bytes 27525120 | tf_op jit(solution)/shard_map/all_to_all | solution.py:85
  71.4 345.4 %copy-start.2 = (bf16[1,64,224]{2,1,0:T(8,128)(2,1)}, bf16[1,64,224]{2,1,0:T(8,128)(2,1)S(1)}, u32[]{:S(2)}) copy-start(bf16[1,64,224]{2,1,0:T(8,128)(2,1)S(1)} %copy.65) | copy-start | bytes 86020
  425.2 3.4 copy-start.1
  479.6 1.0 copy-start
  479.6 1.2 copy-start.8
  545.9 4.6 copy-start.10
  545.9 48.7 %all-to-all-start.4 = ((bf16[8,128,1792]{2,1,0:T(8,128)(2,1)}), bf16[8,128,1792]{2,1,0:T(8,128)(2,1)}, u32[]{:S(2)}, u32[]{:S(2)}) async-start(bf16[8,128,1792]{2,1,0:T(8,128)(2,1)} %bitcast.59), calls=%async_computation.4 | async-start | bytes 7340032 | tf_op jit(solution)/shard_map/all_to_all | solution.py:105
